TPU v7x, 256 devices: a whole 4x4x8 slice. The times are simulated.
256 devices in a mesh: mom: 64 (over x, y, z_lo, core), spin: 4 (over z_hi).
Axes of the slice: x: 4, y: 4, z: 8 (z_hi: 4, z_lo: 2; z = z_hi * 2 + z_lo), core: 2. Of those that a mesh axis runs over, the one named last changes fastest.
Arguments:
- vertex_start: bfloat16 [64, 4, 768, 768], P('mom', 'spin'), may hold values from -6 to 6
- bare_vertex: bfloat16 [64, 4, 768, 768], P('mom', 'spin'), may hold values from -6 to 6
- bubble: bfloat16 [64, 4, 64, 12, 12], P('mom', 'spin'), may hold values from -0.011962891 to 0.011962891
- form_mix: bfloat16 [2, 12, 12], replicated, may hold values from -0.59765625 to 0.59765625
- cross_tables: int32 [2, 64, 64], replicated, may hold values from 0 to 63, as said below
- freq_perm: int32 [2, 64], replicated, may hold values from 0 to 63, each once within a row
Outputs:
- vertex_final: bfloat16 [64, 4, 768, 768], P('mom', 'spin')
Inputs may be any that keep to these rules, and one draw needn't show every extreme that they name: `cross_tables`: for each crossing and frequency, the entries over the 64 momenta are a permutation of the momenta; for each crossing and momentum, every momentum appears exactly once over the 64 frequencies.
All inputs are finite; a program needn't handle non-finite values.
Results may differ from a plain program's by a relative error of at most 0.0085.
Values may be sent and summed in bfloat16 or wider, within the bound.
No kernel may reach another device: no remote copies, remote signals or barrier semaphores. Data moves between devices by JAX's collectives and lax.ppermute only.
A program may use at most 64 MiB of HBM per device.

v0:
```python
import jax
import jax.numpy as jnp
from jax import lax
from jax.sharding import PartitionSpec as P

INNER = 2
COEF_SELF = (-0.5, 0.5, 0.5, 0.5)
COEF_PAIR = (-1.5, -0.5, 1.5, -0.5)


def partner_2(value, axis, stride):
    mask = 2**stride
    pairs = [(source, source ^ mask) for source in range(lax.axis_size(axis))]
    return lax.ppermute(value, axis, pairs)


def make_orders(table, frequency_perm, momentum, momenta, per_peer, freqs):
    freq_range = jnp.arange(freqs, dtype=jnp.int32)
    own_row = jnp.take(table, momentum, axis=0)
    send_order = jnp.argsort(own_row * freqs + freq_range)
    hit_mask = (table == momentum).astype(jnp.int32)
    source = jnp.sum(hit_mask * jnp.arange(momenta, dtype=jnp.int32)[:, None], axis=0)
    within = jnp.sum(hit_mask * (jnp.cumsum(hit_mask, axis=1) - 1), axis=0)
    position = source * per_peer + within
    freq_of = jnp.argsort(frequency_perm)
    return (send_order, jnp.take(position, freq_of, axis=0))


def pack_blocks(matrix, send_order, momenta, per_peer, freqs, forms):
    order_len = matrix.shape[1]
    blocks = jnp.take(matrix.reshape(freqs, forms, order_len), send_order, axis=0)
    return blocks.reshape(momenta, per_peer, forms, order_len)


def unpack_blocks(received, recv_order, mixing, freqs, forms):
    order_len = received.shape[-1]
    gathered = jnp.take(received.reshape(freqs, forms, order_len), recv_order, axis=0)
    mixed = jnp.einsum("lm,fmb->flb", mixing, gathered, preferred_element_type=jnp.float32)
    return mixed.reshape(freqs * forms, order_len)


def local(vertex_start, bare_vertex, bubble, form_mix, cross_tables, freq_perm):
    current = vertex_start[0, 0]
    bare_mat = bare_vertex[0, 0]
    bubble_mat = bubble[0, 0]
    freqs, forms = (bubble_mat.shape[0], bubble_mat.shape[1])
    order_len = current.shape[0]
    momenta = lax.axis_size("mom")
    per_peer = freqs // momenta
    momentum = lax.axis_index("mom")
    channel = lax.axis_index("spin")
    coef_self = jnp.take(jnp.array(COEF_SELF, jnp.float32), channel)
    coef_pair = jnp.take(jnp.array(COEF_PAIR, jnp.float32), channel)
    orders_first = make_orders(cross_tables[0], freq_perm[0], momentum, momenta, per_peer, freqs)
    orders_second = make_orders(cross_tables[1], freq_perm[1], momentum, momenta, per_peer, freqs)
    partner = partner_2(current, "spin", 0)
    stacked = jnp.stack(
        [
            pack_blocks(current, orders_first[0], momenta, per_peer, freqs, forms),
            pack_blocks(partner, orders_first[0], momenta, per_peer, freqs, forms),
            pack_blocks(current, orders_second[0], momenta, per_peer, freqs, forms),
            pack_blocks(partner, orders_second[0], momenta, per_peer, freqs, forms),
        ]
    )
    received = lax.all_to_all(stacked, "mom", split_axis=1, concat_axis=1, tiled=True)
    own_sum = unpack_blocks(received[0], orders_first[1], form_mix[0], freqs, forms)
    own_sum = own_sum + unpack_blocks(received[2], orders_second[1], form_mix[1], freqs, forms)
    other_sum = unpack_blocks(received[1], orders_first[1], form_mix[0], freqs, forms)
    other_sum = other_sum + unpack_blocks(received[3], orders_second[1], form_mix[1], freqs, forms)
    own_round = own_sum.astype(jnp.bfloat16)
    other_round = other_sum.astype(jnp.bfloat16)
    reducible = (
        coef_self * own_round.astype(jnp.float32) + coef_pair * other_round.astype(jnp.float32)
    ).astype(jnp.bfloat16)
    base_sum = bare_mat.astype(jnp.float32) + reducible.astype(jnp.float32)
    for inner_step in range(INNER):
        carried = jnp.einsum(
            "fln,fnb->flb",
            bubble_mat,
            current.reshape(freqs, forms, order_len),
            preferred_element_type=jnp.float32,
        )
        carried = carried.reshape(order_len, order_len).astype(jnp.bfloat16)
        total = base_sum + jnp.dot(bare_mat, carried, preferred_element_type=jnp.float32)
        total = total + jnp.dot(reducible, carried, preferred_element_type=jnp.float32)
        current = total.astype(jnp.bfloat16)
    return current[None, None]


def solution(mesh):
    in_specs = (
        P("mom", "spin", None, None),
        P("mom", "spin", None, None),
        P("mom", "spin", None, None, None),
        P(),
        P(),
        P(),
    )
    out_specs = P("mom", "spin", None, None)
    return jax.shard_map(local, mesh=mesh, in_specs=in_specs, out_specs=out_specs, check_vma=False)
```

profile of v0, /device:TPU:240, one launch (start us, length us, event | category | flops | bytes accessed | tf_op | source)
XLA Modules:
  0.0 203.2 jit_solution(17556819864388075838)
XLA Ops:
  1.5 2.2 %reshape_squeeze.17 = bf16[64,12,768]{2,1,0:T(8,128)(2,1)S(1)} reshape(bf16[1,1,768,768]{3,2,1,0:T(8,128)(2,1)} %param.14) | data formatting | bytes 2359296 | tf_op jit(solution)/shard_map/reshape;squeeze | solution.py:31
  3.7 2.0 %sort.60 = (s32[64]{0:T(128)}, s32[64]{0:T(128)S(1)}) sort(s32[64]{0:T(128)S(1)} %fusion.29, s32[64]{0:T(128)S(1)} %iota.27), dimensions={0}, to_apply=%region_1.0 | sort | flops 384 | bytes 1024 | tf_op jit(solution)/shard_map/jit(argsort)/sort | solution.py:20
  5.8 2.0 %sort.59 = (s32[64]{0:T(128)}, s32[64]{0:T(128)S(1)}) sort(s32[64]{0:T(128)S(1)} %fusion.26, s32[64]{0:T(128)S(1)} %iota.25), dimensions={0}, to_apply=%region_0.0 | sort | flops 384 | bytes 1024 | tf_op jit(solution)/shard_map/jit(argsort)/sort | solution.py:20
  11.4 42.8 %collective-permute-done = bf16[768,768]{1,0:T(8,128)(2,1)} collective-permute-done((bf16[768,768]{1,0:T(8,128)(2,1)}, bf16[768,768]{1,0:T(8,128)(2,1)}, u32[]{:S(2)}, u32[]{:S(2)}) %collective-permute-start) | collective-permute-done | bytes 1179680 | tf_op jit(solution)/shard_map/ppermute | solution.py:14
  54.2 2.2 %reshape.41 = bf16[64,12,768]{2,1,0:T(8,128)(2,1)S(1)} reshape(bf16[768,768]{1,0:T(8,128)(2,1)} %collective-permute-done) | data formatting | bytes 2359296 | tf_op jit(solution)/shard_map/reshape | solution.py:31
  60.0 2.4 %select_bitcast_fusion.1 = (bf16[1,64,1,12,768]{4,3,1,2,0:T(8,128)(2,1)S(1)}, bf16[1,64,1,12,768]{4,3,1,2,0:T(8,128)(2,1)S(1)}) fusion(bf16[64,12,768]{2,1,0:T(8,128)(2,1)} %gather_fusion.2, pred[64]{0:T(512)(128)(4,1)S(1)} %get-tuple-element.99, bf16[64,12,768]{2,1,0:T(8,128)(2,1)} %gather_fusion.3), kind=kLoop, calls=%fused_computation.35 | loop fusion | flops 1179648 | bytes 4718656 | tf_op jit(solution)/shard_map/stack;reshape | solution.py:57
  64.3 8.2 %copy.39 = bf16[4,64,1,12,768]{4,0,3,2,1:T(4,128)(2,1)} copy(bf16[4,64,1,12,768]{4,3,1,2,0:T(8,128)(2,1)S(1)} %pad_maximum_fusion) | data formatting | bytes 9437184 | tf_op jit(solution)/shard_map/stack | solution.py:57
  72.5 9.0 %all-to-all-start = ((bf16[4,64,1,12,768]{4,0,3,2,1:T(4,128)(2,1)}), bf16[4,64,1,12,768]{4,0,3,2,1:T(4,128)(2,1)}, u32[]{:S(2)}, u32[]{:S(2)}) async-start(bf16[4,64,1,12,768]{4,0,3,2,1:T(4,128)(2,1)} %copy.39), calls=%async_computation | async-start | bytes 9437184 | tf_op jit(solution)/shard_map/all_to_all | solution.py:65
  86.7 2.0 %sort.62 = (s32[64]{0:T(128)}, s32[64]{0:T(128)S(1)}) sort(s32[64]{0:T(128)S(1)} %get-tuple-element.89, s32[64]{0:T(128)S(1)} %iota.29), dimensions={0}, to_apply=%region_9.13 | sort | flops 384 | bytes 1024 | tf_op jit(solution)/shard_map/jit(argsort)/sort | solution.py:25
  88.7 2.0 %sort.61 = (s32[64]{0:T(128)}, s32[64]{0:T(128)S(1)}) sort(s32[64]{0:T(128)S(1)} %get-tuple-element.90, s32[64]{0:T(128)S(1)} %iota.28), dimensions={0}, to_apply=%region_5.8 | sort | flops 384 | bytes 1024 | tf_op jit(solution)/shard_map/jit(argsort)/sort | solution.py:25
  92.5 52.2 %all-to-all-done = bf16[4,64,1,12,768]{4,0,3,2,1:T(4,128)(2,1)} async-done(((bf16[4,64,1,12,768]{4,0,3,2,1:T(4,128)(2,1)}), bf16[4,64,1,12,768]{4,0,3,2,1:T(4,128)(2,1)}, u32[]{:S(2)}, u32[]{:S(2)}) %all-to-all-start) | async-done | bytes 4718624 | tf_op jit(solution)/shard_map/all_to_all | solution.py:65
  144.6 15.4 %fusion.36 = (bf16[1,64,1,12,768]{4,0,3,2,1:T(2,128)(2,1)S(1)}, bf16[1,64,1,12,768]{4,0,3,2,1:T(2,128)(2,1)S(1)}, bf16[1,64,1,12,768]{4,0,3,2,1:T(2,128)(2,1)S(1)}, bf16[1,64,1,12,768]{4,0,3,2,1:T(2,128)(2,1)}) fusion(bf16[4,64,1,12,768]{4,0,3,2,1:T(4,128)(2,1)} %all-to-all-done), kind=kLoop, calls=%fused_computation.94 | loop fusion | bytes 9437184 | tf_op jit(solution)/shard_map/slice | solution.py:67
  165.8 2.2 %fusion.5 = f32[64,768,12]{1,2,0:T(8,128)S(1)} fusion(bf16[64,12,768]{2,1,0:T(8,128)(2,1)} %gather_fusion.8, pred[64]{0:T(512)(128)(4,1)S(1)} %get-tuple-element.75, bf16[1,12,12]{2,0,1:T(2,128)(2,1)S(1)} %get-tuple-element.88), kind=kOutput, calls=%fused_computation.29 | convolution fusion | flops 14745600 | bytes 3539296 | tf_op jit(solution)/shard_map/lm,fmb->flb/dot_general | solution.py:38
  168.0 2.3 %fusion.8 = f32[64,768,12]{1,2,0:T(8,128)} fusion(bf16[64,12,768]{2,1,0:T(8,128)(2,1)S(1)} %copy-done.4, pred[64]{0:T(512)(128)(4,1)S(1)} %get-tuple-element.75, bf16[1,12,12]{2,0,1:T(2,128)(2,1)S(1)} %get-tuple-element.88), kind=kOutput, calls=%fused_computation.32 | convolution fusion | flops 14745600 | bytes 3539296 | tf_op jit(solution)/shard_map/lm,fmb->flb/dot_general | solution.py:38
  171.8 3.2 %gather_fusion.7 = bf16[64,12,768]{2,1,0:T(8,128)(2,1)} fusion(bf16[64,12,768]{2,1,0:T(8,128)(2,1)} %bitcast.104, s32[1024]{0:T(1024)S(1)} %pad_clamp_fusion), kind=kCustom, calls=%fused_computation.6.clone | custom fusion | bytes 2359552 | tf_op jit(solution)/shard_map/jit(_take)/gather | solution.py:37
  175.1 3.2 %gather_fusion.9 = bf16[64,12,768]{2,1,0:T(8,128)(2,1)} fusion(bf16[64,12,768]{2,1,0:T(8,128)(2,1)} %bitcast.106, s32[1024]{0:T(1024)S(1)} %pad_clamp_fusion), kind=kCustom, calls=%fused_computation.8.clone | custom fusion | bytes 2359552 | tf_op jit(solution)/shard_map/jit(_take)/gather | solution.py:37
  178.3 2.2 %add_convert_fusion.1 = bf16[64,768,12]{1,2,0:T(8,128)(2,1)S(1)} fusion(f32[64,768,12]{1,2,0:T(8,128)S(1)} %fusion.5, bf16[64,12,768]{2,1,0:T(8,128)(2,1)} %gather_fusion.9, pred[64]{0:T(512)(128)(4,1)S(1)} %get-tuple-element.71, bf16[1,12,12]{2,0,1:T(2,128)(2,1)S(1)} %get-tuple-element.87), kind=kOutput, calls=%fused_computation.13 | convolution fusion | flops 15925248 | bytes 4718944 | tf_op jit(solution)/shard_map/lm,fmb->flb/dot_general | solution.py:38
  182.2 2.1 %convert_bitcast_fusion = f32[64,12,768]{2,1,0:T(8,128)} fusion(bf16[64,768,12]{1,2,0:T(8,128)(2,1)S(1)} %add_convert_fusion), kind=kLoop, calls=%fused_computation.11 | loop fusion | flops 589824 | bytes 3538944 | tf_op jit(solution)/shard_map/convert_element_type | solution.py:75
  185.4 2.6 %reshape.145 = f32[768,768]{1,0:T(8,128)S(1)} reshape(f32[64,12,768]{2,1,0:T(8,128)} %convert_bitcast_fusion) | data formatting | bytes 4718592 | tf_op jit(solution)/shard_map/convert_element_type | solution.py:75
  188.1 3.6 %fusion.38 = f32[768,768]{1,0:T(8,128)S(1)} fusion(bf16[768,768]{1,0:T(8,128)(2,1)} %convert_element_type.94, bf16[768,768]{1,0:T(8,128)(2,1)} %convert_element_type.92), kind=kOutput, calls=%fused_computation.96 | convolution fusion | flops 905969664 | bytes 4718592 | tf_op jit(solution)/shard_map/dot_general | solution.py:85
  191.7 2.2 %fusion.3 = bf16[768,768]{1,0:T(8,128)(2,1)} fusion(f32[768,768]{1,0:T(8,128)S(1)} %fusion.38, bf16[768,768]{1,0:T(8,128)(2,1)S(1)} %copy-done.8, f32[768,768]{1,0:T(8,128)S(1)} %reshape.145, bf16[1,1,768,768]{3,2,1,0:T(8,128)(2,1)S(1)} %copy-done.15), kind=kOutput, calls=%fused_computation.20 | convolution fusion | flops 908918784 | bytes 8257536 | tf_op jit(solution)/shard_map/dot_general | solution.py:84
  193.9 2.2 %reshape.42 = bf16[64,12,768]{2,1,0:T(8,128)(2,1)S(1)} reshape(bf16[768,768]{1,0:T(8,128)(2,1)} %fusion.3) | data formatting | bytes 2359296 | tf_op jit(solution)/shard_map/reshape | solution.py:80
  198.4 2.5 %fusion.39 = f32[768,768]{1,0:T(8,128)S(1)} fusion(bf16[768,768]{1,0:T(8,128)(2,1)S(1)} %copy-done.9, bf16[768,768]{1,0:T(8,128)(2,1)} %convert_element_type.98), kind=kOutput, calls=%fused_computation.97 | convolution fusion | flops 905969664 | bytes 4718592 | tf_op jit(solution)/shard_map/dot_general | solution.py:85
  201.0 2.2 %fusion.15 = bf16[1,1,768,768]{3,2,1,0:T(8,128)(2,1)} fusion(f32[768,768]{1,0:T(8,128)S(1)} %fusion.39, bf16[768,768]{1,0:T(8,128)(2,1)S(1)} %copy-done.10, f32[768,768]{1,0:T(8,128)S(1)} %copy-done.7, bf16[1,1,768,768]{3,2,1,0:T(8,128)(2,1)S(1)} %copy-done.16), kind=kOutput, calls=%fused_computation.43 | convolution fusion | flops 908918784 | bytes 8257536 | tf_op jit(solution)/shard_map/dot_general | solution.py:84
  (88 shorter events, 28.5 us)
Async XLA Ops:
  0.0 3.7 %copy-start.11 = (s32[2,64,64]{2,1,0:T(8,128)S(1)}, s32[2,64,64]{2,1,0:T(8,128)}, u32[]{:S(2)}) copy-start(s32[2,64,64]{2,1,0:T(8,128)} %param.18) | copy-start | bytes 98308
  0.0 54.2 %collective-permute-start = (bf16[768,768]{1,0:T(8,128)(2,1)}, bf16[768,768]{1,0:T(8,128)(2,1)}, u32[]{:S(2)}, u32[]{:S(2)}) collective-permute-start(bf16[768,768]{1,0:T(8,128)(2,1)} %bitcast.108), channel_id=1, source_target_pairs={{0,1},{1,0},{2,3},{3,2},{4,5},{5,4},{6,7},{7,6},{8,9},{9,8},{10,11... | collective-permute-start | bytes 3538952 | tf_op jit(solution)/shard_map/ppermute | solution.py:14
  60.0 2.4 %copy-start.2 = (bf16[64,12,768]{2,1,0:T(8,128)(2,1)S(1)}, bf16[64,12,768]{2,1,0:T(8,128)(2,1)}, u32[]{:S(2)}) copy-start(bf16[64,12,768]{2,1,0:T(8,128)(2,1)} %gather_fusion) | copy-start | bytes 3538948
  60.0 2.8 %copy-start.3 = (bf16[64,12,768]{2,1,0:T(8,128)(2,1)S(1)}, bf16[64,12,768]{2,1,0:T(8,128)(2,1)}, u32[]{:S(2)}) copy-start(bf16[64,12,768]{2,1,0:T(8,128)(2,1)} %gather_fusion.1) | copy-start | bytes 3538948
  72.5 9.1 %copy-start.18 = (f32[4]{0:T(128)S(1)}, f32[4]{0:T(128)}, u32[]{:S(2)}) copy-start(f32[4]{0:T(128)} %constant.83.clone..sunk.2) | copy-start | bytes 52
  72.5 9.7 %copy-start.17 = (f32[4]{0:T(128)S(1)}, f32[4]{0:T(128)}, u32[]{:S(2)}) copy-start(f32[4]{0:T(128)} %constant.82.clone..sunk.2) | copy-start | bytes 52
  72.5 12.1 %copy-start.12 = (bf16[1,1,64,12,12]{2,4,3,1,0:T(8,128)(2,1)S(1)}, bf16[1,1,64,12,12]{2,4,3,1,0:T(8,128)(2,1)}, u32[]{:S(2)}) copy-start(bf16[1,1,64,12,12]{2,4,3,1,0:T(8,128)(2,1)} %param.16) | copy-start | bytes 55300
  72.5 72.1 %all-to-all-start = ((bf16[4,64,1,12,768]{4,0,3,2,1:T(4,128)(2,1)}), bf16[4,64,1,12,768]{4,0,3,2,1:T(4,128)(2,1)}, u32[]{:S(2)}, u32[]{:S(2)}) async-start(bf16[4,64,1,12,768]{4,0,3,2,1:T(4,128)(2,1)} %copy.39), calls=%async_computation | async-start | bytes 9437184 | tf_op jit(solution)/shard_map/all_to_all | solution.py:65
  85.5 1.2 copy-start.14
  85.5 7.0 %copy-start.13 = (bf16[2,12,12]{2,0,1:T(2,128)(2,1)S(1)}, bf16[2,12,12]{2,0,1:T(2,128)(2,1)}, u32[]{:S(2)}) copy-start(bf16[2,12,12]{2,0,1:T(2,128)(2,1)} %param.17) | copy-start | bytes 1732
  165.8 2.2 %copy-start.4 = (bf16[64,12,768]{2,1,0:T(8,128)(2,1)S(1)}, bf16[64,12,768]{2,1,0:T(8,128)(2,1)}, u32[]{:S(2)}) copy-start(bf16[64,12,768]{2,1,0:T(8,128)(2,1)} %gather_fusion.5) | copy-start | bytes 3538948
  168.0 2.3 %copy-start.1 = (bf16[1,64,1,12,768]{4,0,3,2,1:T(2,128)(2,1)S(1)}, bf16[1,64,1,12,768]{4,0,3,2,1:T(2,128)(2,1)}, u32[]{:S(2)}) copy-start(bf16[1,64,1,12,768]{4,0,3,2,1:T(2,128)(2,1)} %get-tuple-element.82) | copy-start | bytes 3538948
  178.3 2.4 %copy-start = (f32[64,768,12]{1,2,0:T(8,128)S(1)}, f32[64,768,12]{1,2,0:T(8,128)}, u32[]{:S(2)}) copy-start(f32[64,768,12]{1,2,0:T(8,128)} %fusion.8) | copy-start | bytes 7077892
  178.3 2.8 %copy-start.5 = (bf16[64,12,768]{2,1,0:T(8,128)(2,1)S(1)}, bf16[64,12,768]{2,1,0:T(8,128)(2,1)}, u32[]{:S(2)}) copy-start(bf16[64,12,768]{2,1,0:T(8,128)(2,1)} %gather_fusion.7) | copy-start | bytes 3538948
  188.0 3.6 %copy-start.6 = (f32[768,768]{1,0:T(8,128)}, f32[768,768]{1,0:T(8,128)S(1)}, u32[]{:S(2)}) copy-start(f32[768,768]{1,0:T(8,128)S(1)} %reshape.145) | copy-start | bytes 7077892
  188.0 3.6 %copy-start.8 = (bf16[768,768]{1,0:T(8,128)(2,1)S(1)}, bf16[768,768]{1,0:T(8,128)(2,1)}, u32[]{:S(2)}) copy-start(bf16[768,768]{1,0:T(8,128)(2,1)} %convert_element_type.92) | copy-start | bytes 3538948
  188.1 3.6 %copy-start.15 = (bf16[1,1,768,768]{3,2,1,0:T(8,128)(2,1)S(1)}, bf16[1,1,768,768]{3,2,1,0:T(8,128)(2,1)}, u32[]{:S(2)}) copy-start(bf16[1,1,768,768]{3,2,1,0:T(8,128)(2,1)} %param.15) | copy-start | bytes 3538948
  196.7 1.7 copy-start.9
  198.4 2.5 %copy-start.7 = (f32[768,768]{1,0:T(8,128)S(1)}, f32[768,768]{1,0:T(8,128)}, u32[]{:S(2)}) copy-start(f32[768,768]{1,0:T(8,128)} %copy-done.6) | copy-start | bytes 7077892
  198.4 2.5 %copy-start.10 = (bf16[768,768]{1,0:T(8,128)(2,1)S(1)}, bf16[768,768]{1,0:T(8,128)(2,1)}, u32[]{:S(2)}) copy-start(bf16[768,768]{1,0:T(8,128)(2,1)} %convert_element_type.98) | copy-start | bytes 3538948
  198.4 2.7 %copy-start.16 = (bf16[1,1,768,768]{3,2,1,0:T(8,128)(2,1)S(1)}, bf16[1,1,768,768]{3,2,1,0:T(8,128)(2,1)}, u32[]{:S(2)}) copy-start(bf16[1,1,768,768]{3,2,1,0:T(8,128)(2,1)} %param.15) | copy-start | bytes 3538948
where the time goes:
time: 204 us; the launch traced here: 203 us
  waiting for transfers between devices  95 us (47%)
  local copies, waits for them, and re-layouts  62 us (30%)
  matrix products  19.4 us (10%)
  other arithmetic  14.7 us (7%)
  starting transfers between devices  10.5 us (5%)
    all_to_all x1, waiting for transfers between devices, local(): lax.all_to_all(stacked, 'mom', split_axis=1, concat_axis=1, tiled=True)  52.2 us
    ppermute x1, waiting for transfers between devices, partner_2(): return lax.ppermute(value, axis, pairs)  42.8 us
    slice x1, local copies, waits for them, and re-layouts, local(): received[2]  15.4 us
    gather x4, local copies, waits for them, and re-layouts, unpack_blocks(): jnp.take(received.reshape(freqs, forms, order_len), recv_order, axis=0)  10 us
    all_to_all x1, starting transfers between devices, local(): lax.all_to_all(stacked, 'mom', split_axis=1, concat_axis=1, tiled=True)  9.03 us
    another operation x1, local copies, waits for them, and re-layouts, local(): jnp.stack([pack_blocks(current, orders_first[0], momenta, per_peer, freqs...  8.24 us
    dot_general x4, matrix products, unpack_blocks(): jnp.einsum('lm,fmb->flb', mixing, gathered, preferred_element_type=jnp.fl...  7.81 us
    gather x4, local copies, waits for them, and re-layouts, pack_blocks(): jnp.take(matrix.reshape(freqs, forms, order_len), send_order, axis=0)  7.2 us
  transfers between devices with their start and end apart: 2, of which 2 were waited for; matrix products, arithmetic and copies ran while one was open for 10% of the time, Pallas kernels for 0%

commit v1 on v0

--- a/solution.py
+++ b/solution.py
@@ -62,7 +62,10 @@
             pack_blocks(partner, orders_second[0], momenta, per_peer, freqs, forms),
         ]
     )
-    received = lax.all_to_all(stacked, "mom", split_axis=1, concat_axis=1, tiled=True)
+    received = jnp.concatenate(
+        lax.all_to_all(jnp.stack(jnp.split(stacked, lax.axis_size("mom"), axis=1)), "mom", 0, 0),
+        axis=1,
+    )
     own_sum = unpack_blocks(received[0], orders_first[1], form_mix[0], freqs, forms)
     own_sum = own_sum + unpack_blocks(received[2], orders_second[1], form_mix[1], freqs, forms)
     other_sum = unpack_blocks(received[1], orders_first[1], form_mix[0], freqs, forms)

time: 204 us -> 185 us (0.907)
  local copies, waits for them, and re-layouts: 62 us -> 48.1 us
  matrix products: 19.4 us -> 15.1 us
    slice x1 -> x0, local copies, waits for them, and re-layouts: 15.4 us -> none  [local(): received[2]]
    another operation x4 -> x5, local copies, waits for them, and re-layouts: 3.71 us -> 8.14 us  [unpack_blocks(): received.reshape(freqs, forms, order_len)]
    all_to_all x0 -> x1, local copies, waits for them, and re-layouts: none -> 3.91 us  [local(): lax.all_to_all(jnp.stack(jnp.split(stacked, lax.axis_size('mom'), axis=1)...]
    gather x4, local copies, waits for them, and re-layouts: 10 us -> 6.28 us  [unpack_blocks(): jnp.take(received.reshape(freqs, forms, order_len), recv_order, axis=0)]
    another operation x1 -> x2, local copies, waits for them, and re-layouts: 8.24 us -> 4.61 us  [local(): jnp.stack(jnp.split(stacked, lax.axis_size('mom'), axis=1))]
    dot_general x4, matrix products: 7.81 us -> 4.57 us  [unpack_blocks(): jnp.einsum('lm,fmb->flb', mixing, gathered, preferred_element_type=jnp.fl...]
  transfers between devices with their start and end apart: 2 -> 2, of which waited for: 2 -> 2; matrix products, arithmetic and copies ran while one was open for 10% -> 11% of each run, Pallas kernels for 0% -> 0%
where the time goes in v1:
time: 185 us
  waiting for transfers between devices  94.2 us (51%)
  local copies, waits for them, and re-layouts  48.1 us (26%)
  matrix products  15.1 us (8%)
  other arithmetic  14.7 us (8%)
  starting transfers between devices  10.5 us (6%)
  between operations  2.22 us (1%)
    all_to_all x1, waiting for transfers between devices, local(): lax.all_to_all(jnp.stack(jnp.split(stacked, lax.axis_size('mom'), axis=1)...  52.2 us
    ppermute x1, waiting for transfers between devices, partner_2(): return lax.ppermute(value, axis, pairs)  42 us
    all_to_all x1, starting transfers between devices, local(): lax.all_to_all(jnp.stack(jnp.split(stacked, lax.axis_size('mom'), axis=1)...  9.05 us
    another operation x5, local copies, waits for them, and re-layouts, unpack_blocks(): received.reshape(freqs, forms, order_len)  8.14 us
    gather x4, local copies, waits for them, and re-layouts, pack_blocks(): jnp.take(matrix.reshape(freqs, forms, order_len), send_order, axis=0)  7.2 us
    gather x4, local copies, waits for them, and re-layouts, unpack_blocks(): jnp.take(received.reshape(freqs, forms, order_len), recv_order, axis=0)  6.28 us
    dot_general x2, matrix products, local(): jnp.dot(reducible, carried, preferred_element_type=jnp.float32)  5.02 us
    another operation x2, local copies, waits for them, and re-layouts, local(): jnp.stack(jnp.split(stacked, lax.axis_size('mom'), axis=1))  4.61 us
  transfers between devices with their start and end apart: 2, of which 2 were waited for; matrix products, arithmetic and copies ran while one was open for 11% of the time, Pallas kernels for 0%

profile of v1, /device:TPU:240, one launch (start us, length us, event | category | flops | bytes accessed | tf_op | source)
XLA Modules:
  0.0 184.8 jit_solution(17708618855114819446)
XLA Ops:
  1.5 2.2 %reshape_squeeze.17 = bf16[64,12,768]{2,1,0:T(8,128)(2,1)S(1)} reshape(bf16[1,1,768,768]{3,2,1,0:T(8,128)(2,1)} %param.14) | data formatting | bytes 2359296 | tf_op jit(solution)/shard_map/reshape;squeeze | solution.py:31
  4.5 2.0 %sort.60 = (s32[64]{0:T(128)}, s32[64]{0:T(128)S(1)}) sort(s32[64]{0:T(128)S(1)} %fusion.29, s32[64]{0:T(128)S(1)} %iota.27), dimensions={0}, to_apply=%region_1.0 | sort | flops 384 | bytes 1024 | tf_op jit(solution)/shard_map/jit(argsort)/sort | solution.py:20
  6.5 2.0 %sort.59 = (s32[64]{0:T(128)}, s32[64]{0:T(128)S(1)}) sort(s32[64]{0:T(128)S(1)} %fusion.26, s32[64]{0:T(128)S(1)} %iota.25), dimensions={0}, to_apply=%region_0.0 | sort | flops 384 | bytes 1024 | tf_op jit(solution)/shard_map/jit(argsort)/sort | solution.py:20
  12.2 42.0 %collective-permute-done = bf16[768,768]{1,0:T(8,128)(2,1)} collective-permute-done((bf16[768,768]{1,0:T(8,128)(2,1)}, bf16[768,768]{1,0:T(8,128)(2,1)}, u32[]{:S(2)}, u32[]{:S(2)}) %collective-permute-start) | collective-permute-done | bytes 1179680 | tf_op jit(solution)/shard_map/ppermute | solution.py:14
  54.2 2.2 %reshape.53 = bf16[64,12,768]{2,1,0:T(8,128)(2,1)S(1)} reshape(bf16[768,768]{1,0:T(8,128)(2,1)} %collective-permute-done) | data formatting | bytes 2359296 | tf_op jit(solution)/shard_map/reshape | solution.py:31
  58.2 1.8 gather_fusion.3
  60.0 2.4 %select_bitcast_fusion.1 = (bf16[1,64,1,12,768]{4,3,1,2,0:T(8,128)(2,1)S(1)}, bf16[1,64,1,12,768]{4,3,1,2,0:T(8,128)(2,1)S(1)}) fusion(bf16[64,12,768]{2,1,0:T(8,128)(2,1)} %gather_fusion.2, pred[64]{0:T(512)(128)(4,1)S(1)} %get-tuple-element.99, bf16[64,12,768]{2,1,0:T(8,128)(2,1)} %gather_fusion.3), kind=kLoop, calls=%fused_computation.32 | loop fusion | flops 1179648 | bytes 4718656 | tf_op jit(solution)/shard_map/stack;reshape | solution.py:57
  65.4 4.6 %copy.351 = bf16[64,4,1,1,12,768]{5,1,4,3,2,0:T(4,128)(2,1)} copy(bf16[64,4,1,1,12,768]{5,4,1,3,2,0:T(8,128)(2,1)S(1)} %constant_dynamic-update-slice_fusion) | data formatting | bytes 9437184 | tf_op jit(solution)/shard_map/stack | solution.py:66
  70.0 9.0 %all-to-all-start = ((bf16[64,4,1,1,12,768]{5,1,4,3,2,0:T(4,128)(2,1)}), bf16[64,4,1,1,12,768]{5,1,4,3,2,0:T(4,128)(2,1)}, u32[]{:S(2)}, u32[]{:S(2)}) async-start(bf16[64,4,1,1,12,768]{5,1,4,3,2,0:T(4,128)(2,1)} %copy.351), calls=%async_computation | async-start | bytes 9437184 | tf_op jit(solution)/shard_map/all_to_all | solution.py:66
  84.1 2.0 %sort.62 = (s32[64]{0:T(128)}, s32[64]{0:T(128)S(1)}) sort(s32[64]{0:T(128)S(1)} %get-tuple-element.89, s32[64]{0:T(128)S(1)} %iota.29), dimensions={0}, to_apply=%region_9.13 | sort | flops 384 | bytes 1024 | tf_op jit(solution)/shard_map/jit(argsort)/sort | solution.py:25
  86.2 2.0 %sort.61 = (s32[64]{0:T(128)}, s32[64]{0:T(128)S(1)}) sort(s32[64]{0:T(128)S(1)} %get-tuple-element.90, s32[64]{0:T(128)S(1)} %iota.28), dimensions={0}, to_apply=%region_5.8 | sort | flops 384 | bytes 1024 | tf_op jit(solution)/shard_map/jit(argsort)/sort | solution.py:25
  89.9 52.2 %all-to-all-done = bf16[64,4,1,1,12,768]{5,1,4,3,2,0:T(4,128)(2,1)} async-done(((bf16[64,4,1,1,12,768]{5,1,4,3,2,0:T(4,128)(2,1)}), bf16[64,4,1,1,12,768]{5,1,4,3,2,0:T(4,128)(2,1)}, u32[]{:S(2)}, u32[]{:S(2)}) %all-to-all-start) | async-done | bytes 4718624 | tf_op jit(solution)/shard_map/all_to_all | solution.py:66
  142.1 3.9 %copy.435 = bf16[64,4,1,1,12,768]{5,0,4,3,2,1:T(8,128)(2,1)S(1)} copy(bf16[64,4,1,1,12,768]{5,1,4,3,2,0:T(4,128)(2,1)} %all-to-all-done) | data formatting | bytes 9437184 | tf_op jit(solution)/shard_map/all_to_all | solution.py:66
  151.6 1.9 %copy.357 = bf16[64,12,768]{2,1,0:T(8,128)(2,1)S(1)} copy(bf16[64,12,768]{2,0,1:T(8,128)(2,1)} %get-tuple-element.81) | data formatting | bytes 2359296 | tf_op jit(solution)/shard_map/reshape;squeeze | solution.py:37
  153.6 3.1 %copy.353 = bf16[64,12,768]{2,1,0:T(8,128)(2,1)} copy(bf16[64,12,768]{2,0,1:T(8,128)(2,1)} %get-tuple-element.82) | data formatting | bytes 2359296 | tf_op jit(solution)/shard_map/reshape;squeeze | solution.py:37
  158.4 2.1 %gather_fusion.5 = bf16[64,12,768]{2,1,0:T(8,128)(2,1)S(1)} fusion(bf16[64,12,768]{2,1,0:T(8,128)(2,1)} %copy.353, s32[1024]{0:T(1024)S(1)} %pad_clamp_fusion.2), kind=kCustom, calls=%fused_computation.5.clone | custom fusion | bytes 2359552 | tf_op jit(solution)/shard_map/jit(_take)/gather | solution.py:37
  160.5 2.1 %fusion.5 = f32[64,768,12]{1,2,0:T(8,128)S(1)} fusion(bf16[64,12,768]{2,1,0:T(8,128)(2,1)} %gather_fusion.8, pred[64]{0:T(512)(128)(4,1)S(1)} %get-tuple-element.75, bf16[1,12,12]{2,0,1:T(2,128)(2,1)S(1)} %get-tuple-element.88), kind=kOutput, calls=%fused_computation.26 | convolution fusion | flops 14745600 | bytes 3539296 | tf_op jit(solution)/shard_map/lm,fmb->flb/dot_general | solution.py:38
  165.1 2.1 %convert_bitcast_fusion = f32[64,12,768]{2,1,0:T(8,128)} fusion(bf16[64,768,12]{1,2,0:T(8,128)(2,1)S(1)} %add_convert_fusion), kind=kLoop, calls=%fused_computation.12 | loop fusion | flops 589824 | bytes 3538944 | tf_op jit(solution)/shard_map/convert_element_type | solution.py:78
  168.3 3.9 %reshape.158 = f32[768,768]{1,0:T(8,128)} reshape(f32[64,12,768]{2,1,0:T(8,128)} %convert_bitcast_fusion) | data formatting | bytes 4718592 | tf_op jit(solution)/shard_map/convert_element_type | solution.py:78
  172.3 2.5 %fusion.37 = f32[768,768]{1,0:T(8,128)S(1)} fusion(bf16[768,768]{1,0:T(8,128)(2,1)} %convert_element_type.94, bf16[768,768]{1,0:T(8,128)(2,1)S(1)} %copy-done.5), kind=kOutput, calls=%fused_computation.224 | convolution fusion | flops 905969664 | bytes 4718592 | tf_op jit(solution)/shard_map/dot_general | solution.py:88
  174.8 2.2 %fusion.3 = bf16[768,768]{1,0:T(8,128)(2,1)} fusion(f32[768,768]{1,0:T(8,128)S(1)} %fusion.37, bf16[768,768]{1,0:T(8,128)(2,1)S(1)} %copy-done.5, f32[768,768]{1,0:T(8,128)S(1)} %copy-done.3, bf16[1,1,768,768]{3,2,1,0:T(8,128)(2,1)S(1)} %copy-done.10), kind=kOutput, calls=%fused_computation.21 | convolution fusion | flops 908918784 | bytes 8257536 | tf_op jit(solution)/shard_map/dot_general | solution.py:87
  177.1 2.2 %reshape.55 = bf16[64,12,768]{2,1,0:T(8,128)(2,1)S(1)} reshape(bf16[768,768]{1,0:T(8,128)(2,1)} %fusion.3) | data formatting | bytes 2359296 | tf_op jit(solution)/shard_map/reshape | solution.py:83
  180.1 2.5 %fusion.38 = f32[768,768]{1,0:T(8,128)S(1)} fusion(bf16[768,768]{1,0:T(8,128)(2,1)} %convert_element_type.94, bf16[768,768]{1,0:T(8,128)(2,1)S(1)} %convert_element_type.98), kind=kOutput, calls=%fused_computation.225 | convolution fusion | flops 905969664 | bytes 4718592 | tf_op jit(solution)/shard_map/dot_general | solution.py:88
  182.7 2.2 %fusion.15 = bf16[1,1,768,768]{3,2,1,0:T(8,128)(2,1)} fusion(f32[768,768]{1,0:T(8,128)S(1)} %fusion.38, bf16[768,768]{1,0:T(8,128)(2,1)S(1)} %convert_element_type.98, f32[768,768]{1,0:T(8,128)S(1)} %copy-done.4, bf16[1,1,768,768]{3,2,1,0:T(8,128)(2,1)S(1)} %copy-done.11), kind=kOutput, calls=%fused_computation.40 | convolution fusion | flops 908918784 | bytes 8257536 | tf_op jit(solution)/shard_map/dot_general | solution.py:87
  (143 shorter events, 27.4 us)
Async XLA Ops:
  0.0 54.2 %collective-permute-start = (bf16[768,768]{1,0:T(8,128)(2,1)}, bf16[768,768]{1,0:T(8,128)(2,1)}, u32[]{:S(2)}, u32[]{:S(2)}) collective-permute-start(bf16[768,768]{1,0:T(8,128)(2,1)} %bitcast.482), channel_id=1, source_target_pairs={{0,1},{1,0},{2,3},{3,2},{4,5},{5,4},{6,7},{7,6},{8,9},{9,8},{10,11... | collective-permute-start | bytes 3538952 | tf_op jit(solution)/shard_map/ppermute | solution.py:14
  60.0 2.4 %copy-start = (bf16[64,12,768]{2,1,0:T(8,128)(2,1)S(1)}, bf16[64,12,768]{2,1,0:T(8,128)(2,1)}, u32[]{:S(2)}) copy-start(bf16[64,12,768]{2,1,0:T(8,128)(2,1)} %gather_fusion) | copy-start | bytes 3538948
  60.0 2.8 %copy-start.1 = (bf16[64,12,768]{2,1,0:T(8,128)(2,1)S(1)}, bf16[64,12,768]{2,1,0:T(8,128)(2,1)}, u32[]{:S(2)}) copy-start(bf16[64,12,768]{2,1,0:T(8,128)(2,1)} %gather_fusion.1) | copy-start | bytes 3538948
  69.9 9.1 %copy-start.13 = (f32[4]{0:T(128)S(1)}, f32[4]{0:T(128)}, u32[]{:S(2)}) copy-start(f32[4]{0:T(128)} %constant.83.clone..sunk.2) | copy-start | bytes 52
  70.0 9.7 %copy-start.12 = (f32[4]{0:T(128)S(1)}, f32[4]{0:T(128)}, u32[]{:S(2)}) copy-start(f32[4]{0:T(128)} %constant.82.clone..sunk.2) | copy-start | bytes 52
  70.0 11.7 %copy-start.6 = (s32[2,64,64]{2,1,0:T(8,128)S(1)}, s32[2,64,64]{2,1,0:T(8,128)}, u32[]{:S(2)}) copy-start(s32[2,64,64]{2,1,0:T(8,128)} %param.18) | copy-start | bytes 98308
  70.0 12.2 %copy-start.7 = (bf16[1,1,64,12,12]{2,4,3,1,0:T(8,128)(2,1)S(1)}, bf16[1,1,64,12,12]{2,4,3,1,0:T(8,128)(2,1)}, u32[]{:S(2)}) copy-start(bf16[1,1,64,12,12]{2,4,3,1,0:T(8,128)(2,1)} %param.16) | copy-start | bytes 55300
  70.0 14.2 %copy-start.9 = (s32[2,64]{1,0:T(2,128)S(1)}, s32[2,64]{1,0:T(2,128)}, u32[]{:S(2)}) copy-start(s32[2,64]{1,0:T(2,128)} %param.19) | copy-start | bytes 1540
  70.0 72.1 %all-to-all-start = ((bf16[64,4,1,1,12,768]{5,1,4,3,2,0:T(4,128)(2,1)}), bf16[64,4,1,1,12,768]{5,1,4,3,2,0:T(4,128)(2,1)}, u32[]{:S(2)}, u32[]{:S(2)}) async-start(bf16[64,4,1,1,12,768]{5,1,4,3,2,0:T(4,128)(2,1)} %copy.351), calls=%async_computation | async-start | bytes 9437184 | tf_op jit(solution)/shard_map/all_to_all | solution.py:66
  79.0 10.9 %copy-start.8 = (bf16[2,12,12]{2,0,1:T(2,128)(2,1)S(1)}, bf16[2,12,12]{2,0,1:T(2,128)(2,1)}, u32[]{:S(2)}) copy-start(bf16[2,12,12]{2,0,1:T(2,128)(2,1)} %param.17) | copy-start | bytes 1732
  162.5 1.5 copy-start.2
  165.1 7.2 %copy-start.5 = (bf16[768,768]{1,0:T(8,128)(2,1)S(1)}, bf16[768,768]{1,0:T(8,128)(2,1)}, u32[]{:S(2)}) copy-start(bf16[768,768]{1,0:T(8,128)(2,1)} %convert_element_type.92) | copy-start | bytes 3538948
  168.3 6.5 %copy-start.10 = (bf16[1,1,768,768]{3,2,1,0:T(8,128)(2,1)S(1)}, bf16[1,1,768,768]{3,2,1,0:T(8,128)(2,1)}, u32[]{:S(2)}) copy-start(bf16[1,1,768,768]{3,2,1,0:T(8,128)(2,1)} %param.15) | copy-start | bytes 3538948
  172.3 2.5 %copy-start.3 = (f32[768,768]{1,0:T(8,128)S(1)}, f32[768,768]{1,0:T(8,128)}, u32[]{:S(2)}) copy-start(f32[768,768]{1,0:T(8,128)} %reshape.158) | copy-start | bytes 7077892
  180.1 2.5 %copy-start.4 = (f32[768,768]{1,0:T(8,128)S(1)}, f32[768,768]{1,0:T(8,128)}, u32[]{:S(2)}) copy-start(f32[768,768]{1,0:T(8,128)} %reshape.158) | copy-start | bytes 7077892
  180.1 2.5 %copy-start.11 = (bf16[1,1,768,768]{3,2,1,0:T(8,128)(2,1)S(1)}, bf16[1,1,768,768]{3,2,1,0:T(8,128)(2,1)}, u32[]{:S(2)}) copy-start(bf16[1,1,768,768]{3,2,1,0:T(8,128)(2,1)} %param.15) | copy-start | bytes 3538948
